TPU v7x, 512 devices: a whole 4x8x8 slice. The times are simulated.
512 devices in a mesh: segment: 16 (over z, core), mp: 32 (over y, x).
Axes of the slice: x: 4, y: 8, z: 8, core: 2. Of those that a mesh axis runs over, the one named last changes fastest.
Arguments:
- rows: bfloat16 [16, 2, 128, 8192], P('segment', None, None, 'mp'), may hold values from -6 to 6
- carry: bfloat16 [16, 128, 8192], P('segment', None, 'mp'), may hold values from -6 to 6
- weights: bfloat16 [16, 2, 8192, 4096], P('segment', None, None, 'mp'), may hold values from -1.1932427 to 1.1932427
- neighbours: int32 [16, 2, 2, 2], P('segment'), may hold values from 0 to 7, all different within a row
Outputs:
- passed: bfloat16 [16, 128, 8192], P('segment', None, 'mp')
- returned: bfloat16 [16, 128, 8192], P('segment', None, 'mp')
- kv_grad: bfloat16 [1024, 2, 4096], P(None, None, 'mp')
Inputs may be any that keep to these rules, and one draw needn't show every extreme that they name: Each group's 2 neighbours are different pool blocks; pool blocks are numbered by encoder segment in order, then by row.
All inputs are finite; a program needn't handle non-finite values.
Results may differ from a plain program's by a relative error of at most 0.02.
The roundings to bfloat16 on the way count: a program that leaves them out, or rounds other values in their place, can miss the bound.
Values may be sent and summed in bfloat16 or wider, within the bound.
No kernel may reach another device: no remote copies, remote signals or barrier semaphores. Data moves between devices by JAX's collectives and lax.ppermute only.
A program may use at most 64 MiB of HBM per device.

v0:
```python
import math
import jax
import jax.numpy as jnp
from jax import lax
from jax.sharding import PartitionSpec as P

GROUP = 64
NBLEN = 128
NEIGH = 2


def from_behind(x, axis, by):
    devices = lax.axis_size(axis)
    return lax.ppermute(x, axis, [(i, (i + by) % devices) for i in range(devices)])


def attend(queries, key_rows, score_scale):
    scores = (
        jnp.einsum("cqd,ckd->cqk", queries, key_rows, preferred_element_type=jnp.float32)
        * score_scale
    )
    soft = jax.nn.softmax(scores, axis=-1)
    return (soft, soft.astype(jnp.bfloat16))


def attend_back(queries, key_rows, value_rows, soft, rounded, upstream, score_scale):
    d_soft = jnp.einsum("cqd,ckd->cqk", upstream, value_rows, preferred_element_type=jnp.float32)
    grad_values = jnp.einsum("cqk,cqd->ckd", rounded, upstream, preferred_element_type=jnp.float32)
    d_scores = soft * (d_soft - jnp.sum(d_soft * soft, axis=-1, keepdims=True))
    grad_queries = (
        jnp.einsum("cqk,ckd->cqd", d_scores, key_rows.astype(jnp.float32)) * score_scale
    ).astype(jnp.bfloat16)
    grad_keys = jnp.einsum("cqk,cqd->ckd", d_scores, queries.astype(jnp.float32)) * score_scale
    return (grad_queries, grad_keys, grad_values)


def per_device(rows, carry, weights, neighbours):
    segments = lax.axis_size("segment")
    encoders = segments // 4
    first_encoder = segments - encoders
    is_encoder = lax.axis_index("segment") >= first_encoder
    local_rows = rows[0]
    local_carry = carry[0]
    full_rows, full_carry = (
        lax.all_gather(local_rows, "mp", axis=2, tiled=True),
        lax.all_gather(local_carry, "mp", axis=1, tiled=True),
    )
    tokens = local_rows.shape[1]
    width = full_rows.shape[2]
    head = weights.shape[3]
    w_query = weights[0, 0]
    w_out = weights[0, 1]

    def encode():
        flat = full_rows.reshape(2 * tokens, width)
        keyval = jnp.concatenate(
            [
                jnp.dot(flat, w_query, preferred_element_type=jnp.float32),
                jnp.dot(flat, w_out, preferred_element_type=jnp.float32),
            ],
            axis=-1,
        ).astype(jnp.bfloat16)
        return (keyval, jnp.zeros((2 * tokens, head), jnp.bfloat16))

    def decode():
        queries = jnp.dot(
            full_rows.reshape(2 * tokens, width), w_query, preferred_element_type=jnp.float32
        ).astype(jnp.bfloat16)
        return (jnp.zeros((2 * tokens, 2 * head), jnp.bfloat16), queries)

    encoded, queries = lax.cond(is_encoder, encode, decode)
    per_encoder = 2 * tokens // NBLEN
    pool_blocks = encoders * per_encoder
    collected = lax.all_gather(encoded, "segment", axis=0, tiled=True)
    pool = collected[first_encoder * 2 * tokens :].reshape(pool_blocks, NBLEN, 2 * head)
    groups = tokens // GROUP
    local_nbr = neighbours[0]
    score_scale = 1.0 / math.sqrt(head)
    query_blocks = queries.reshape(2, groups, GROUP, head)

    def fetch(batch):
        picked = pool[local_nbr[batch]].reshape(groups, NEIGH * NBLEN, 2 * head)
        return (picked[..., :head], picked[..., head:])

    keys_fwd, values_fwd = fetch(0)
    soft_fwd, rounded_fwd = attend(query_blocks[0], keys_fwd, score_scale)
    mixed = jnp.einsum(
        "cqk,ckd->cqd", rounded_fwd, values_fwd, preferred_element_type=jnp.float32
    ).astype(jnp.bfloat16)
    mixed_flat = mixed.reshape(tokens, head)
    piece = w_out
    out_sum = (
        lax.psum_scatter(
            lax.dot_general(
                piece, mixed_flat, (((1,), (1,)), ((), ())), preferred_element_type=jnp.float32
            ).astype(jnp.bfloat16),
            "mp",
            scatter_dimension=0,
            tiled=True,
        )
        .astype(jnp.float32)
        .T
    )
    forward_rows = (local_rows[0].astype(jnp.float32) + out_sum).astype(jnp.bfloat16)
    forward_rows = jnp.where(is_encoder, local_carry, forward_rows)
    passed = from_behind(forward_rows[None], "segment", 1)
    upstream = (
        jnp.dot(full_carry, w_out, preferred_element_type=jnp.float32)
        .astype(jnp.bfloat16)
        .reshape(groups, GROUP, head)
    )
    keys_back, values_back = fetch(1)
    soft_back, rounded_back = attend(query_blocks[1], keys_back, score_scale)
    grad_queries, grad_keys, grad_values = attend_back(
        query_blocks[1], keys_back, values_back, soft_back, rounded_back, upstream, score_scale
    )
    grad_flat = grad_queries.reshape(tokens, head)
    piece = w_query
    grad_input = (
        lax.psum_scatter(
            lax.dot_general(
                piece, grad_flat, (((1,), (1,)), ((), ())), preferred_element_type=jnp.float32
            ).astype(jnp.bfloat16),
            "mp",
            scatter_dimension=0,
            tiled=True,
        )
        .astype(jnp.float32)
        .T
    )
    back = local_carry.astype(jnp.float32) + grad_input
    back_rows = jnp.where(is_encoder, local_carry, back.astype(jnp.bfloat16))
    returned = from_behind(back_rows[None], "segment", -1)
    onehot = (
        local_nbr[1][..., None] == jnp.arange(pool_blocks, dtype=jnp.int32)[None, None, :]
    ).astype(jnp.float32)
    grad_keyval = jnp.concatenate([grad_keys, grad_values], axis=-1).reshape(
        groups, NEIGH, NBLEN, 2 * head
    )
    contrib = jnp.einsum("cbp,cbrf->prf", onehot, grad_keyval)
    contrib = jnp.where(is_encoder, jnp.zeros_like(contrib), contrib)
    pooled = lax.psum(contrib.astype(jnp.bfloat16), "segment").astype(jnp.float32)
    kv_grad = pooled.reshape(pool_blocks * NBLEN, 2, head).astype(jnp.bfloat16)
    return (passed, returned, kv_grad)


def solution(mesh):
    placed = (
        P("segment", None, None, "mp"),
        P("segment", None, "mp"),
        P("segment", None, None, "mp"),
        P("segment", None, None, None),
    )
    return jax.shard_map(
        per_device,
        mesh=mesh,
        in_specs=placed,
        out_specs=(P("segment", None, "mp"), P("segment", None, "mp"), P(None, None, "mp")),
        check_vma=False,
    )
```

profile of v0, /device:TPU:1, one launch (start us, length us, event | category | flops | bytes accessed | tf_op | source)
XLA Modules:
  0.0 812.3 jit_solution(813906581693303927)
XLA Ops:
  7.2 0.7 all-gather.8.cloned.1.call-update
  7.9 0.7 all-gather.10.cloned.1.call-update
  8.7 3.8 slice_bitcast_fusion
  12.5 89.2 %all-gather.8.cloned.1.call-done = bf16[1,2,128,8192]{3,2,1,0:T(8,128)(2,1)} async-done(((bf16[1,2,128,256]{3,2,1,0:T(8,128)(2,1)}), bf16[1,2,128,8192]{3,2,1,0:T(8,128)(2,1)}) %all-gather.8.cloned.1.call-update) | async-done | bytes 4194320 | tf_op jit(solution)/shard_map/all_gather | solution.py:45
  101.8 3.5 conditional.1
  101.8 3.4 convolution_convert_fusion
  105.3 0.6 copy-done.1
  106.1 79.5 %all-gather.10.cloned.1.call-done = bf16[1,128,8192]{2,1,0:T(8,128)(2,1)} async-done(((bf16[1,128,256]{2,1,0:T(8,128)(2,1)}), bf16[1,128,8192]{2,1,0:T(8,128)(2,1)}) %all-gather.10.cloned.1.call-update) | async-done | bytes 2097168 | tf_op jit(solution)/shard_map/all_gather | solution.py:46
  185.7 2.9 fusion.13
  188.6 45.9 %all-gather.6.cloned.1.call-done = bf16[4096,256]{1,0:T(8,128)(2,1)} async-done(((bf16[256,256]{1,0:T(8,128)(2,1)}), bf16[4096,256]{1,0:T(8,128)(2,1)}) %all-gather.6.cloned.1.call-update) | async-done | bytes 2097168 | tf_op jit(solution)/shard_map/all_gather | solution.py:74
  234.5 1.1 slice.67
  235.6 0.6 gather_fusion.1
  236.3 0.4 fusion.37
  236.9 0.3 fusion.12
  237.3 3.7 fusion.3
  241.1 0.6 gather_fusion
  242.0 0.3 convolution_convert_fusion.5
  242.4 3.6 fusion.2
  246.1 0.3 fusion.28
  246.5 0.4 convolution_multiply_fusion
  247.0 0.5 copy.12
  247.5 0.5 fusion.7
  248.0 0.6 copy.13
  248.6 1.0 convert_element_type.80
  249.6 205.3 %reduce-scatter.5.cloned.1.call-done = bf16[256,128]{0,1:T(8,128)(2,1)} async-done(((bf16[8192,128]{0,1:T(8,128)(2,1)}), bf16[256,128]{0,1:T(8,128)(2,1)}) %reduce-scatter.5.cloned.1.call-update) | async-done | bytes 65552 | tf_op jit(solution)/shard_map/reduce_scatter | solution.py:120
  454.9 224.9 %reduce-scatter.3.cloned.1.call-done = bf16[256,128]{0,1:T(8,128)(2,1)} async-done(((bf16[8192,128]{0,1:T(8,128)(2,1)}), bf16[256,128]{0,1:T(8,128)(2,1)}) %reduce-scatter.3.cloned.1.call-update) | async-done | bytes 65552 | tf_op jit(solution)/shard_map/reduce_scatter | solution.py:93
  679.8 0.9 fusion.25
  680.7 6.9 collective-permute-start
  687.6 114.5 %all-reduce.2.cloned.1.call-done = bf16[1024,2,128]{0,2,1:T(8,128)(2,1)} async-done(((bf16[1024,2,128]{0,2,1:T(8,128)(2,1)}), bf16[1024,2,128]{0,2,1:T(8,128)(2,1)}) %all-reduce.2.cloned.1.call-update) | async-done | bytes 524304 | tf_op jit(solution)/shard_map/psum | solution.py:142
  802.1 2.0 copy.14
  804.1 0.6 copy.25
  804.8 0.6 copy.26
  (35 shorter events, 1.5 us)
Async XLA Ops:
  7.2 94.6 %all-gather.8.cloned.1.call-start = ((), (), s32[]{:S(2)}) async-start(), calls=%async_computation.6 | async-start | bytes 4325376 | tf_op jit(solution)/shard_map/all_gather | solution.py:45
  7.9 177.8 %all-gather.10.cloned.1.call-start = ((), (), s32[]{:S(2)}) async-start(), calls=%async_computation.7 | async-start | bytes 2162688 | tf_op jit(solution)/shard_map/all_gather | solution.py:46
  8.6 225.9 %all-gather.6.cloned.1.call-start = ((), (), s32[]{:S(2)}) async-start(), calls=%async_computation.2 | async-start | bytes 2228224 | tf_op jit(solution)/shard_map/all_gather | solution.py:74
  101.8 4.2 copy-start.4
  105.3 0.7 copy-start.1
  106.0 348.9 %reduce-scatter.5.cloned.1.call-start = ((), (), s32[]{:S(2)}) async-start(), calls=%async_computation.4 | async-start | bytes 2162688 | tf_op jit(solution)/shard_map/reduce_scatter | solution.py:120
  241.0 438.8 %reduce-scatter.3.cloned.1.call-start = ((), (), s32[]{:S(2)}) async-start(), calls=%async_computation.3 | async-start | bytes 2162688 | tf_op jit(solution)/shard_map/reduce_scatter | solution.py:93
  246.0 556.2 %all-reduce.2.cloned.1.call-start = ((), (), s32[]{:S(2)}) async-start(), calls=%async_computation.5 | async-start | bytes 1048576 | tf_op jit(solution)/shard_map/psum | solution.py:142
  247.5 432.3 %copy-start.2 = (bf16[1,2,128,256]{3,2,1,0:T(8,128)(2,1)S(1)}, bf16[1,2,128,256]{3,2,1,0:T(8,128)(2,1)}, u32[]{:S(2)}) copy-start(bf16[1,2,128,256]{3,2,1,0:T(8,128)(2,1)} %param.6) | copy-start | bytes 393220
  247.5 432.3 %copy-start.3 = (bf16[1,128,256]{2,1,0:T(8,128)(2,1)S(1)}, bf16[1,128,256]{2,1,0:T(8,128)(2,1)}, u32[]{:S(2)}) copy-start(bf16[1,128,256]{2,1,0:T(8,128)(2,1)} %param.7) | copy-start | bytes 196612
  680.7 123.5 %collective-permute-start = (bf16[1,128,256]{2,1,0:T(8,128)(2,1)S(1)}, bf16[1,128,256]{2,1,0:T(8,128)(2,1)S(1)}, u32[]{:S(2)}, u32[]{:S(2)}) collective-permute-start(bf16[1,128,256]{2,1,0:T(8,128)(2,1)S(1)} %get-tuple-element.53), channel_id=1, source_target_pairs={{0,32},{32,64},{64,96},{96,128},{128,160},{160,192},{192,224},{224... | collective-permute-start | bytes 196616 | tf_op jit(solution)/shard_map/ppermute | solution.py:14
  687.6 116.5 %collective-permute-start.1 = (bf16[1,128,256]{2,1,0:T(8,128)(2,1)S(1)}, bf16[1,128,256]{2,1,0:T(8,128)(2,1)S(1)}, u32[]{:S(2)}, u32[]{:S(2)}) collective-permute-start(bf16[1,128,256]{2,1,0:T(8,128)(2,1)S(1)} %get-tuple-element.52), channel_id=1, source_target_pairs={{0,480},{32,0},{64,32},{96,64},{128,96},{160,128},{192,160},{224,1... | collective-permute-start | bytes 196616 | tf_op jit(solution)/shard_map/ppermute | solution.py:14
Sparse Core Ops, SparseCore 0:
  11.0 90.6 all-gather.7
  104.8 80.7 all-gather.9
  188.4 46.0 all-gather.5
  241.1 213.7 reduce-scatter.4
  459.8 219.9 reduce-scatter.2
  682.5 119.5 all-reduce.1
where the time goes:
time: 813 us; the launch traced here: 812 us
  waiting for transfers between devices  761 us (94%)
  matrix products  16.1 us (2%)
  between operations  14.3 us (2%)
  local copies, waits for them, and re-layouts  12.4 us (2%)
    reduce_scatter x1, waiting for transfers between devices, per_device(): lax.psum_scatter(lax.dot_general(piece, mixed_flat, (((1,), (1,)), ((), (...  225 us
    reduce_scatter x1, waiting for transfers between devices, per_device(): lax.psum_scatter(lax.dot_general(piece, grad_flat, (((1,), (1,)), ((), ()...  205 us
    psum x1, waiting for transfers between devices, per_device(): lax.psum(contrib.astype(jnp.bfloat16), 'segment').astype(jnp.float32)  115 us
    all_gather x1, waiting for transfers between devices, per_device(): lax.all_gather(local_rows, 'mp', axis=2, tiled=True)  89.2 us
    all_gather x1, waiting for transfers between devices, per_device(): lax.all_gather(local_carry, 'mp', axis=1, tiled=True)  79.5 us
    all_gather x1, waiting for transfers between devices, per_device(): collected = lax.all_gather(encoded, 'segment', axis=0, tiled=True)  45.9 us
  transfers between devices with their start and end apart: 8, of which 6 were waited for; matrix products, arithmetic and copies ran while one was open for 3% of the time, Pallas kernels for 0%

commit v1 on v0

--- a/solution.py
+++ b/solution.py
@@ -35,6 +35,15 @@
 
 
 def per_device(rows, carry, weights, neighbours):
+
+    def detail_unit_all(array_here):
+        lane_axis = "mp"
+        full_n = lax.axis_size(lane_axis)
+        x_new = range(array_here.ndim)
+        p_next = map(lambda h: full_n if h == 1 else 1, x_new)
+        found_now = jnp.tile(array_here, list(p_next))
+        return lax.all_to_all(found_now, lane_axis, split_axis=1, concat_axis=1, tiled=True)
+
     segments = lax.axis_size("segment")
     encoders = segments // 4
     first_encoder = segments - encoders
@@ -43,7 +52,7 @@
     local_carry = carry[0]
     full_rows, full_carry = (
         lax.all_gather(local_rows, "mp", axis=2, tiled=True),
-        lax.all_gather(local_carry, "mp", axis=1, tiled=True),
+        detail_unit_all(local_carry),
     )
     tokens = local_rows.shape[1]
     width = full_rows.shape[2]

time: 813 us -> 752 us (0.925)
  waiting for transfers between devices: 761 us -> 684 us
  starting transfers between devices: 7.19 us -> 17.8 us
    all_gather x1 -> x0, waiting for transfers between devices: 79.5 us -> none  [per_device(): lax.all_gather(local_carry, 'mp', axis=1, tiled=True)]
    all_to_all x0 -> x1, starting transfers between devices: none -> 10.6 us  [detail_unit_all(): lax.all_to_all(found_now, lane_axis, split_axis=1, concat_axis=1, tiled=T...]
  transfers between devices with their start and end apart: 8 -> 8, of which waited for: 6 -> 5; matrix products, arithmetic and copies ran while one was open for 3% -> 4% of each run, Pallas kernels for 0% -> 0%
where the time goes in v1:
time: 752 us; the launch traced here: 751 us
  waiting for transfers between devices  684 us (91%)
  local copies, waits for them, and re-layouts  18.1 us (2%)
  starting transfers between devices  17.8 us (2%)
  matrix products  15.5 us (2%)
  between operations  13.9 us (2%)
    reduce_scatter x1, waiting for transfers between devices, per_device(): lax.psum_scatter(lax.dot_general(piece, mixed_flat, (((1,), (1,)), ((), (...  225 us
    reduce_scatter x1, waiting for transfers between devices, per_device(): lax.psum_scatter(lax.dot_general(piece, grad_flat, (((1,), (1,)), ((), ()...  205 us
    psum x1, waiting for transfers between devices, per_device(): lax.psum(contrib.astype(jnp.bfloat16), 'segment').astype(jnp.float32)  115 us
    all_gather x1, waiting for transfers between devices, per_device(): lax.all_gather(local_rows, 'mp', axis=2, tiled=True)  95.9 us
    all_gather x1, waiting for transfers between devices, per_device(): collected = lax.all_gather(encoded, 'segment', axis=0, tiled=True)  43 us
  transfers between devices with their start and end apart: 8, of which 5 were waited for; matrix products, arithmetic and copies ran while one was open for 4% of the time, Pallas kernels for 0%

profile of v1, /device:TPU:1, one launch (start us, length us, event | category | flops | bytes accessed | tf_op | source)
XLA Modules:
  0.0 751.1 jit_solution(16535631230419899332)
XLA Ops:
  7.2 0.7 all-gather.6.cloned.1.call-update
  7.9 2.4 tile.2
  10.3 10.6 %all-to-all-start = ((bf16[128,32,256]{2,0,1:T(8,128)(2,1)}), bf16[128,32,256]{2,0,1:T(8,128)(2,1)}, u32[]{:S(2)}, u32[]{:S(2)}) async-start(bf16[128,32,256]{2,0,1:T(8,128)(2,1)} %tile.2), calls=%async_computation.1 | async-start | bytes 4194304 | tf_op jit(solution)/shard_map/all_to_all | solution.py:45
  21.0 3.9 slice_bitcast_fusion
  24.9 95.9 %all-gather.6.cloned.1.call-done = bf16[1,2,128,8192]{3,2,1,0:T(8,128)(2,1)} async-done(((bf16[1,2,128,256]{3,2,1,0:T(8,128)(2,1)}), bf16[1,2,128,8192]{3,2,1,0:T(8,128)(2,1)}) %all-gather.6.cloned.1.call-update) | async-done | bytes 4194320 | tf_op jit(solution)/shard_map/all_gather | solution.py:54
  120.8 3.5 conditional.1
  120.8 3.4 convolution_convert_fusion
  124.3 0.6 copy-done.1
  125.1 3.2 copy.21
  128.4 2.3 convolution_convert_fusion.5
  130.7 43.0 %all-gather.4.cloned.1.call-done = bf16[4096,256]{1,0:T(8,128)(2,1)} async-done(((bf16[256,256]{1,0:T(8,128)(2,1)}), bf16[4096,256]{1,0:T(8,128)(2,1)}) %all-gather.4.cloned.1.call-update) | async-done | bytes 2097168 | tf_op jit(solution)/shard_map/all_gather | solution.py:83
  173.7 1.1 slice.67
  174.8 0.6 gather_fusion.1
  175.5 0.4 fusion.32
  176.2 0.3 fusion.10
  176.5 3.7 fusion.3
  180.3 0.6 gather_fusion
  181.6 3.6 fusion.2
  185.3 0.3 fusion.23
  185.7 0.4 convolution_multiply_fusion
  186.2 0.5 copy.23
  186.7 0.5 fusion.5
  187.2 0.6 copy.24
  187.8 1.0 convert_element_type.80
  188.8 205.2 %reduce-scatter.5.cloned.1.call-done = bf16[256,128]{0,1:T(8,128)(2,1)} async-done(((bf16[8192,128]{0,1:T(8,128)(2,1)}), bf16[256,128]{0,1:T(8,128)(2,1)}) %reduce-scatter.5.cloned.1.call-update) | async-done | bytes 65552 | tf_op jit(solution)/shard_map/reduce_scatter | solution.py:129
  394.1 224.9 %reduce-scatter.3.cloned.1.call-done = bf16[256,128]{0,1:T(8,128)(2,1)} async-done(((bf16[8192,128]{0,1:T(8,128)(2,1)}), bf16[256,128]{0,1:T(8,128)(2,1)}) %reduce-scatter.3.cloned.1.call-update) | async-done | bytes 65552 | tf_op jit(solution)/shard_map/reduce_scatter | solution.py:102
  619.0 0.9 fusion.20
  619.9 6.9 collective-permute-start
  626.8 114.5 %all-reduce.2.cloned.1.call-done = bf16[1024,2,128]{0,2,1:T(8,128)(2,1)} async-done(((bf16[1024,2,128]{0,2,1:T(8,128)(2,1)}), bf16[1024,2,128]{0,2,1:T(8,128)(2,1)}) %all-reduce.2.cloned.1.call-update) | async-done | bytes 524304 | tf_op jit(solution)/shard_map/psum | solution.py:151
  741.3 2.0 copy.25
  743.3 0.6 copy.36
  744.0 0.6 copy.37
  (36 shorter events, 1.8 us)
Async XLA Ops:
  7.2 113.6 %all-gather.6.cloned.1.call-start = ((), (), s32[]{:S(2)}) async-start(), calls=%async_computation.7 | async-start | bytes 4325376 | tf_op jit(solution)/shard_map/all_gather | solution.py:54
  10.3 114.8 %all-to-all-start = ((bf16[128,32,256]{2,0,1:T(8,128)(2,1)}), bf16[128,32,256]{2,0,1:T(8,128)(2,1)}, u32[]{:S(2)}, u32[]{:S(2)}) async-start(bf16[128,32,256]{2,0,1:T(8,128)(2,1)} %tile.2), calls=%async_computation.1 | async-start | bytes 4194304 | tf_op jit(solution)/shard_map/all_to_all | solution.py:45
  21.0 152.7 %all-gather.4.cloned.1.call-start = ((), (), s32[]{:S(2)}) async-start(), calls=%async_computation.3 | async-start | bytes 2228224 | tf_op jit(solution)/shard_map/all_gather | solution.py:83
  120.8 4.2 copy-start.4
  124.3 0.7 copy-start.1
  125.0 269.1 %reduce-scatter.5.cloned.1.call-start = ((), (), s32[]{:S(2)}) async-start(), calls=%async_computation.5 | async-start | bytes 2162688 | tf_op jit(solution)/shard_map/reduce_scatter | solution.py:129
  180.2 438.8 %reduce-scatter.3.cloned.1.call-start = ((), (), s32[]{:S(2)}) async-start(), calls=%async_computation.4 | async-start | bytes 2162688 | tf_op jit(solution)/shard_map/reduce_scatter | solution.py:102
  185.2 556.1 %all-reduce.2.cloned.1.call-start = ((), (), s32[]{:S(2)}) async-start(), calls=%async_computation.6 | async-start | bytes 1048576 | tf_op jit(solution)/shard_map/psum | solution.py:151
  186.7 432.3 %copy-start.2 = (bf16[1,2,128,256]{3,2,1,0:T(8,128)(2,1)S(1)}, bf16[1,2,128,256]{3,2,1,0:T(8,128)(2,1)}, u32[]{:S(2)}) copy-start(bf16[1,2,128,256]{3,2,1,0:T(8,128)(2,1)} %param.6) | copy-start | bytes 393220
  186.7 432.3 %copy-start.3 = (bf16[1,128,256]{2,1,0:T(8,128)(2,1)S(1)}, bf16[1,128,256]{2,1,0:T(8,128)(2,1)}, u32[]{:S(2)}) copy-start(bf16[1,128,256]{2,1,0:T(8,128)(2,1)} %param.7) | copy-start | bytes 196612
  619.9 123.4 %collective-permute-start = (bf16[1,128,256]{2,1,0:T(8,128)(2,1)S(1)}, bf16[1,128,256]{2,1,0:T(8,128)(2,1)S(1)}, u32[]{:S(2)}, u32[]{:S(2)}) collective-permute-start(bf16[1,128,256]{2,1,0:T(8,128)(2,1)S(1)} %get-tuple-element.65), channel_id=1, source_target_pairs={{0,32},{32,64},{64,96},{96,128},{128,160},{160,192},{192,224},{224... | collective-permute-start | bytes 196616 | tf_op jit(solution)/shard_map/ppermute | solution.py:14
  626.8 116.5 %collective-permute-start.1 = (bf16[1,128,256]{2,1,0:T(8,128)(2,1)S(1)}, bf16[1,128,256]{2,1,0:T(8,128)(2,1)S(1)}, u32[]{:S(2)}, u32[]{:S(2)}) collective-permute-start(bf16[1,128,256]{2,1,0:T(8,128)(2,1)S(1)} %get-tuple-element.64), channel_id=1, source_target_pairs={{0,480},{32,0},{64,32},{96,64},{128,96},{160,128},{192,160},{224,1... | collective-permute-start | bytes 196616 | tf_op jit(solution)/shard_map/ppermute | solution.py:14
Sparse Core Ops, SparseCore 0:
  11.0 109.7 all-gather.5
  125.1 48.5 all-gather.3
  180.3 213.7 reduce-scatter.4
  399.0 219.9 reduce-scatter.2
  621.7 119.5 all-reduce.1
